TPU v7x, 32 devices: a whole 2x2x4 slice. The times are simulated.
32 devices in a mesh: crop: 8 (over z, y), head: 4 (over x, core).
Axes of the slice: x: 2, y: 2, z: 4, core: 2. Of those that a mesh axis runs over, the one named last changes fastest.
Arguments:
- global_rows: bfloat16 [4096, 4096], P('crop', 'head'), may hold values from -6 to 6
- crop_tokens: bfloat16 [8192, 4096], P('crop', 'head'), may hold values from -6 to 6
- query_weight: bfloat16 [4096, 4096], P('crop', 'head'), may hold values from -0.125 to 0.125
- key_weight: bfloat16 [4096, 4096], P('crop', 'head'), may hold values from -0.125 to 0.125
- value_weight: bfloat16 [4096, 4096], P('crop', 'head'), may hold values from -0.09375 to 0.09375
- fetch_slots: int32 [8, 8, 2], P('crop'), may hold values from 0 to 63
- region_slots: int32 [128, 8], P('crop'), may hold values from 0 to 15, as said below
- region_len: int32 [128], P('crop'), may hold values from 4 to 8
Outputs:
- attended: bfloat16 [4096, 4096], P('crop', 'head')
Inputs may be any that keep to these rules, and one draw needn't show every extreme that they name: `fetch_slots`: entry [s, o, c] numbers one of the 64 crop blocks of index s of crop. `region_slots`: the blocks listed for one page-row are distinct; the lists of the 16 page-rows of one index of crop together name all 16 delivered blocks. page-row r uses its first region_len[r] listed blocks.
All inputs are finite; a program needn't handle non-finite values.
Results may differ from a plain program's by a relative error of at most 0.008.
Values may be sent and summed in bfloat16 or wider, within the bound.
No kernel may reach another device: no remote copies, remote signals or barrier semaphores. Data moves between devices by JAX's collectives and lax.ppermute only.
A program may use at most 128 MiB of HBM per device.

v0:
```python
import jax
import jax.numpy as jnp
from jax import lax
from jax.sharding import PartitionSpec as P

HD = 128
CT = 16
CAP = 2
NB = 8
GR = 32


def add_rows(left, piece):
    return jnp.dot(left, piece, preferred_element_type=jnp.float32)


def body(
    global_rows,
    crop_tokens,
    query_weight,
    key_weight,
    value_weight,
    fetch_slots,
    region_slots,
    region_len,
):
    width = key_weight.shape[1]
    heads_here = width // HD
    ncrop = lax.axis_size("crop")
    rows_here = region_slots.shape[0]
    queries_in = lax.all_gather(global_rows, "head", axis=1, tiled=True)
    query = add_rows(queries_in, lax.all_gather(query_weight, "crop", axis=0, tiled=True)).astype(
        jnp.bfloat16
    )
    picks = fetch_slots[0]
    tokens_all = lax.all_gather(crop_tokens, "head", axis=1, tiled=True)

    def add_one(piece):
        return add_rows(tokens_all, piece)

    keys_full = add_one(lax.all_gather(key_weight, "crop", axis=0, tiled=True))
    vals_full = add_one(lax.all_gather(value_weight, "crop", axis=0, tiled=True))
    packed = jnp.concatenate(
        [keys_full.astype(jnp.bfloat16), vals_full.astype(jnp.bfloat16)], axis=1
    )
    packed = packed.reshape(-1, CT, 2 * width)
    outgoing = packed[picks]
    incoming = lax.all_to_all(outgoing, "crop", split_axis=0, concat_axis=0, tiled=True)
    slotted = incoming.reshape(ncrop * CAP, CT, 2 * width)
    listed = slotted[region_slots].reshape(rows_here, NB * CT, 2 * width)
    keys_row = listed[:, :, :width].reshape(rows_here, NB * CT, heads_here, HD)
    vals_row = listed[:, :, width:].reshape(rows_here, NB * CT, heads_here, HD)
    query_row = query.reshape(rows_here, GR, heads_here, HD)
    scale = 1.0 / HD**0.5
    scores = (
        jnp.einsum("rghe,rkhe->rhgk", query_row, keys_row, preferred_element_type=jnp.float32)
        * scale
    )
    used = (jnp.arange(NB * CT, dtype=jnp.int32) // CT)[None, :] < region_len[:, None]
    scores = jnp.where(used[:, None, None, :], scores, jnp.float32(-1e30))
    top = jnp.max(scores, axis=-1, keepdims=True)
    expo = jnp.exp(scores - top)
    weights = (expo / jnp.sum(expo, axis=-1, keepdims=True)).astype(jnp.bfloat16)
    result = jnp.einsum("rhgk,rkhe->rghe", weights, vals_row, preferred_element_type=jnp.float32)
    return result.astype(jnp.bfloat16).reshape(rows_here * GR, width)


def solution(mesh):
    placed = (
        P("crop", "head"),
        P("crop", "head"),
        P("crop", "head"),
        P("crop", "head"),
        P("crop", "head"),
        P("crop", None, None),
        P("crop", None),
        P("crop"),
    )
    return jax.shard_map(
        body, mesh=mesh, in_specs=placed, out_specs=P("crop", "head"), check_vma=False
    )
```

profile of v0, /device:TPU:0, one launch (start us, length us, event | category | flops | bytes accessed | tf_op | source)
XLA Modules:
  0.0 549.0 jit_solution(13589215673044014440)
XLA Ops:
  6.5 0.0 copy-start.2
  6.5 0.0 copy-start.1
  6.5 0.0 all-gather.6.cloned.1.call-start
  6.5 0.7 all-gather.6.cloned.1.call-update
  7.3 0.0 all-gather.8.cloned.1.call-start
  7.3 0.7 all-gather.8.cloned.1.call-update
  8.0 0.0 all-gather.10.cloned.1.call-start
  8.1 0.7 all-gather.10.cloned.1.call-update
  8.7 0.0 all-gather.12.cloned.1.call-start
  8.8 0.5 all-gather.12.cloned.1.call-update
  9.3 0.0 all-gather.14.cloned.1.call-start
  9.4 0.5 all-gather.14.cloned.1.call-update
  9.9 0.0 copy-done.2
  9.9 0.1 copy.13
  10.0 0.1 reshape.96
  10.1 0.0 copy-done.1
  10.1 0.1 copy.14
  10.2 0.1 reshape.104
  10.3 59.6 %all-gather.6.cloned.1.call-done = bf16[1024,4096]{1,0:T(8,128)(2,1)} async-done(((bf16[1024,1024]{1,0:T(8,128)(2,1)}), bf16[1024,4096]{1,0:T(8,128)(2,1)}) %all-gather.6.cloned.1.call-update) | async-done | bytes 8388624 | tf_op jit(solution)/shard_map/all_gather | solution.py:36
  69.9 127.1 %all-gather.8.cloned.1.call-done = bf16[4096,1024]{1,0:T(8,128)(2,1)} async-done(((bf16[512,1024]{1,0:T(8,128)(2,1)}), bf16[4096,1024]{1,0:T(8,128)(2,1)}) %all-gather.8.cloned.1.call-update) | async-done | bytes 8388624 | tf_op jit(solution)/shard_map/all_gather | solution.py:41
  197.0 13.7 %convolution_convert_fusion.1 = bf16[1024,1024]{0,1:T(8,128)(2,1)S(1)} fusion(bf16[1024,4096]{1,0:T(8,128)(2,1)} %all-gather.6.cloned.1.call-done, bf16[4096,1024]{1,0:T(8,128)(2,1)} %all-gather.8.cloned.1.call-done), kind=kOutput, calls=%fused_computation.8 | convolution fusion | flops 8590983168 | bytes 18874368 | tf_op jit(solution)/shard_map/dot_general | solution.py:14
  210.8 111.5 %all-gather.10.cloned.1.call-done = bf16[4096,1024]{1,0:T(8,128)(2,1)} async-done(((bf16[512,1024]{1,0:T(8,128)(2,1)}), bf16[4096,1024]{1,0:T(8,128)(2,1)}) %all-gather.10.cloned.1.call-update) | async-done | bytes 8388624 | tf_op jit(solution)/shard_map/all_gather | solution.py:42
  322.3 13.7 %convolution_convert_fusion = bf16[1024,1024]{0,1:T(8,128)(2,1)S(1)} fusion(bf16[1024,4096]{1,0:T(8,128)(2,1)} %all-gather.6.cloned.1.call-done, bf16[4096,1024]{1,0:T(8,128)(2,1)} %all-gather.10.cloned.1.call-done), kind=kOutput, calls=%fused_computation.7 | convolution fusion | flops 8590983168 | bytes 18874368 | tf_op jit(solution)/shard_map/dot_general | solution.py:14
  336.1 2.4 pad_maximum_fusion
  338.5 6.6 %copy.12 = bf16[1024,2048]{1,0:T(8,128)(2,1)} copy(bf16[1024,2048]{0,1:T(8,128)(2,1)} %pad_maximum_fusion) | data formatting | bytes 8388608 | tf_op jit(solution)/shard_map/concatenate | solution.py:43
  345.1 0.0 copy-start.3
  345.1 3.8 gather_fusion
  348.9 3.7 all-to-all-start
  352.6 0.0 copy-done.3
  352.6 0.1 broadcast_compare_fusion
  352.7 3.7 all-gather.12.cloned.1.call-done
  356.4 133.9 %all-gather.14.cloned.1.call-done = bf16[4096,1024]{1,0:T(8,128)(2,1)} async-done(((bf16[512,1024]{1,0:T(8,128)(2,1)}), bf16[4096,1024]{1,0:T(8,128)(2,1)}) %all-gather.14.cloned.1.call-update) | async-done | bytes 8388624 | tf_op jit(solution)/shard_map/all_gather | solution.py:32
  490.3 9.1 %fusion.3 = bf16[64,8,8,128]{3,1,2,0:T(8,128)(2,1)S(1)} fusion(bf16[512,4096]{1,0:T(8,128)(2,1)} %all-gather.12.cloned.1.call-done, bf16[4096,1024]{1,0:T(8,128)(2,1)} %all-gather.14.cloned.1.call-done), kind=kOutput, calls=%fused_computation.13 | convolution fusion | flops 4295491584 | bytes 13631488 | tf_op jit(solution)/shard_map/dot_general | solution.py:14
  499.4 0.3 copy.23
  499.7 0.0 all-to-all-done
  499.7 6.2 %gather_fusion.1 = bf16[128,16,2048]{2,1,0:T(8,128)(2,1)} fusion(bf16[16,16,2048]{2,1,0:T(8,128)(2,1)S(1)} %bitcast.29, s32[1024]{0:T(1024)S(1)} %pad_clamp_fusion), kind=kCustom, calls=%fused_computation.1 | custom fusion | bytes 16777728 | tf_op jit(solution)/shard_map/gather | solution.py:50
  506.0 6.0 %fusion.17 = (bf16[16,128,1024]{2,1,0:T(8,128)(2,1)}, bf16[16,128,1024]{2,1,0:T(8,128)(2,1)}) fusion(bf16[16,128,2048]{2,1,0:T(8,128)(2,1)} %bitcast.30), kind=kLoop, calls=%fused_computation.35 | loop fusion | bytes 16777216 | tf_op jit(solution)/shard_map/slice | solution.py:51
  512.0 6.4 %copy.16 = bf16[16,128,1024]{1,2,0:T(8,128)(2,1)} copy(bf16[16,128,1024]{2,1,0:T(8,128)(2,1)} %get-tuple-element.5) | data formatting | bytes 8388608 | tf_op jit(solution)/shard_map/slice | solution.py:51
  518.4 6.4 %copy.15 = bf16[16,128,1024]{1,2,0:T(8,128)(2,1)} copy(bf16[16,128,1024]{2,1,0:T(8,128)(2,1)} %get-tuple-element.6) | data formatting | bytes 8388608 | tf_op jit(solution)/shard_map/slice | solution.py:52
  524.8 3.4 fusion.4
  528.2 0.0 copy-start
  528.2 1.3 copy-done
  529.5 1.2 fusion.18
  530.7 10.1 %fusion.2 = bf16[16,32,8,128]{3,1,2,0:T(8,128)(2,1)S(1)} fusion(bf16[16,128,8,128]{1,3,2,0:T(8,128)(2,1)} %bitcast.34, f32[16,8,32]{2,1,0:T(8,128)S(1)} %fusion.18, f32[16,8,32,128]{3,2,1,0:T(8,128)} %copy-done, pred[16,128]{1,0:T(8,128)(4,1)S(1)} %broadcast_compare_fusion), kind=kOutput, calls=%fused_computation.12 | convolution fusion | flops 137367680 | bytes 7358464 | tf_op jit(solution)/shard_map/rhgk,rkhe->rghe/dot_general | solution.py:64
  540.8 0.5 copy.20
  541.2 1.2 copy.28
  (5 shorter events, 0.0 us)
Async XLA Ops:
  6.5 3.4 copy-start.2
  6.5 3.6 copy-start.1
  6.5 63.4 %all-gather.6.cloned.1.call-start = ((), (), s32[]{:S(2)}) async-start(), calls=%async_computation.1 | async-start | bytes 10485760 | tf_op jit(solution)/shard_map/all_gather | solution.py:36
  7.3 189.8 %all-gather.8.cloned.1.call-start = ((), (), s32[]{:S(2)}) async-start(), calls=%async_computation.2 | async-start | bytes 9437184 | tf_op jit(solution)/shard_map/all_gather | solution.py:41
  8.0 314.3 %all-gather.10.cloned.1.call-start = ((), (), s32[]{:S(2)}) async-start(), calls=%async_computation.3 | async-start | bytes 9437184 | tf_op jit(solution)/shard_map/all_gather | solution.py:42
  8.7 347.7 %all-gather.12.cloned.1.call-start = ((), (), s32[]{:S(2)}) async-start(), calls=%async_computation.4 | async-start | bytes 5242880 | tf_op jit(solution)/shard_map/all_gather | solution.py:31
  9.3 481.0 %all-gather.14.cloned.1.call-start = ((), (), s32[]{:S(2)}) async-start(), calls=%async_computation.5 | async-start | bytes 9437184 | tf_op jit(solution)/shard_map/all_gather | solution.py:32
  345.1 7.5 %copy-start.3 = (s32[16]{0:T(128)S(1)}, s32[16]{0:T(128)}, u32[]{:S(2)}) copy-start(s32[16]{0:T(128)} %param.15) | copy-start | bytes 196
  348.9 150.9 %all-to-all-start = ((bf16[8,2,16,2048]{3,2,1,0:T(8,128)(2,1)}), bf16[8,2,16,2048]{3,2,1,0:T(8,128)(2,1)S(1)}, u32[]{:S(2)}, u32[]{:S(2)}) async-start(bf16[8,2,16,2048]{3,2,1,0:T(8,128)(2,1)} %bitcast.2), calls=%async_computation | async-start | bytes 2097152 | tf_op jit(solution)/shard_map/all_to_all | solution.py:48
  528.2 1.3 copy-start
Sparse Core Ops, SparseCore 0:
  8.9 60.9 all-gather.5
  72.1 124.9 all-gather.7
  199.2 123.1 all-gather.9
  323.7 32.6 all-gather.11
  358.4 131.8 all-gather.13
where the time goes:
time: 550 us; the launch traced here: 549 us
  waiting for transfers between devices  439 us (80%)
  matrix products  50.1 us (9%)
  local copies, waits for them, and re-layouts  39.1 us (7%)
  between operations  13.3 us (2%)
    all_gather x1, waiting for transfers between devices, body(): lax.all_gather(query_weight, 'crop', axis=0, tiled=True)  134 us
    all_gather x1, waiting for transfers between devices, body(): keys_full = add_one(lax.all_gather(key_weight, 'crop', axis=0, tiled=True))  127 us
    all_gather x1, waiting for transfers between devices, body(): lax.all_gather(value_weight, 'crop', axis=0, tiled=True)  112 us
    all_gather x1, waiting for transfers between devices, body(): tokens_all = lax.all_gather(crop_tokens, 'head', axis=1, tiled=True)  59.6 us
    dot_general x3, matrix products, add_rows(): return jnp.dot(left, piece, preferred_element_type=jnp.float32)  36.6 us
    slice x2, local copies, waits for them, and re-layouts, body(): keys_row = listed[:, :, :width].reshape(rows_here, NB * CT, heads_here, HD)  12.4 us
  transfers between devices with their start and end apart: 6, of which 5 were waited for; matrix products, arithmetic and copies ran while one was open for 9% of the time, Pallas kernels for 0%

commit v1 on v0

--- a/solution.py
+++ b/solution.py
@@ -33,7 +33,13 @@
         jnp.bfloat16
     )
     picks = fetch_slots[0]
-    tokens_all = lax.all_gather(crop_tokens, "head", axis=1, tiled=True)
+    size = lax.axis_size("head")
+    block, blocks = (crop_tokens, [crop_tokens])
+    for _ in range(size - 1):
+        block = lax.ppermute(block, "head", [(i, (i + 1) % size) for i in range(size)])
+        blocks.insert(0, block)
+    line = jnp.concatenate(blocks, axis=1)
+    tokens_all = jnp.roll(line, (lax.axis_index("head") + 1) * crop_tokens.shape[1], axis=1)
 
     def add_one(piece):
         return add_rows(tokens_all, piece)

time: 550 us -> 490 us (0.89)
  waiting for transfers between devices: 439 us -> 360 us
  local copies, waits for them, and re-layouts: 39.1 us -> 57.6 us
    all_gather x1, waiting for transfers between devices: 127 us -> 31.6 us  [body(): keys_full = add_one(lax.all_gather(key_weight, 'crop', axis=0, tiled=True))]
    ppermute x0 -> x3, waiting for transfers between devices: none -> 76.8 us  [body(): lax.ppermute(block, 'head', [(i, (i + 1) % size) for i in range(size)])]
    all_gather x1 -> x0, waiting for transfers between devices: 59.6 us -> none  [body(): tokens_all = lax.all_gather(crop_tokens, 'head', axis=1, tiled=True)]
    unnamed x10 -> x19, local copies, waits for them, and re-layouts: 2.86 us -> 19.9 us
  transfers between devices with their start and end apart: 6 -> 8, of which waited for: 5 -> 7; matrix products, arithmetic and copies ran while one was open for 9% -> 14% of each run, Pallas kernels for 0% -> 0%
where the time goes in v1:
time: 490 us; the launch traced here: 489 us
  waiting for transfers between devices  360 us (73%)
  local copies, waits for them, and re-layouts  57.6 us (12%)
  matrix products  50.1 us (10%)
  between operations  13.3 us (3%)
    all_gather x1, waiting for transfers between devices, body(): lax.all_gather(query_weight, 'crop', axis=0, tiled=True)  134 us
    all_gather x1, waiting for transfers between devices, body(): lax.all_gather(value_weight, 'crop', axis=0, tiled=True)  112 us
    ppermute x3, waiting for transfers between devices, body(): lax.ppermute(block, 'head', [(i, (i + 1) % size) for i in range(size)])  76.8 us
    dot_general x3, matrix products, add_rows(): return jnp.dot(left, piece, preferred_element_type=jnp.float32)  36.7 us
    all_gather x1, waiting for transfers between devices, body(): keys_full = add_one(lax.all_gather(key_weight, 'crop', axis=0, tiled=True))  31.6 us
    unnamed x19, local copies, waits for them, and re-layouts  19.9 us
    slice x2, local copies, waits for them, and re-layouts, body(): keys_row = listed[:, :, :width].reshape(rows_here, NB * CT, heads_here, HD)  12.4 us
    dot_general x1, matrix products, body(): jnp.einsum('rhgk,rkhe->rghe', weights, vals_row, preferred_element_type=j...  10.1 us
  transfers between devices with their start and end apart: 8, of which 7 were waited for; matrix products, arithmetic and copies ran while one was open for 14% of the time, Pallas kernels for 0%

profile of v1, /device:TPU:0, one launch (start us, length us, event | category | flops | bytes accessed | tf_op | source)
XLA Modules:
  0.0 489.1 jit_solution(3052027532606891487)
XLA Ops:
  6.5 0.0 copy-start.3
  6.5 0.0 copy-start.2
  6.5 0.0 all-gather.5.cloned.1.call-start
  6.5 0.7 all-gather.5.cloned.1.call-update
  7.3 0.0 all-gather.7.cloned.1.call-start
  7.3 0.7 all-gather.7.cloned.1.call-update
  8.0 0.0 all-gather.9.cloned.1.call-start
  8.1 0.7 all-gather.9.cloned.1.call-update
  8.7 0.0 all-gather.11.cloned.1.call-start
  8.8 0.5 all-gather.11.cloned.1.call-update
  9.3 0.5 collective-permute-start
  9.8 25.9 %collective-permute-done = bf16[1024,1024]{1,0:T(8,128)(2,1)S(1)} collective-permute-done((bf16[1024,1024]{1,0:T(8,128)(2,1)}, bf16[1024,1024]{1,0:T(8,128)(2,1)S(1)}, u32[]{:S(2)}, u32[]{:S(2)}) %collective-permute-start) | collective-permute-done | bytes 2097184 | tf_op jit(solution)/shard_map/ppermute | solution.py:39
  35.7 0.0 collective-permute-start.1
  35.7 25.5 %collective-permute-done.1 = bf16[1024,1024]{1,0:T(8,128)(2,1)} collective-permute-done((bf16[1024,1024]{1,0:T(8,128)(2,1)S(1)}, bf16[1024,1024]{1,0:T(8,128)(2,1)}, u32[]{:S(2)}, u32[]{:S(2)}) %collective-permute-start.1) | collective-permute-done | bytes 2097184 | tf_op jit(solution)/shard_map/ppermute | solution.py:39
  61.2 0.0 collective-permute-start.2
  61.3 0.0 copy-done.3
  61.3 0.1 copy.13
  61.3 0.1 reshape.96
  61.4 0.0 copy-done.2
  61.4 0.1 copy.14
  61.5 0.1 reshape.104
  61.6 25.4 %collective-permute-done.2 = bf16[1024,1024]{1,0:T(8,128)(2,1)} collective-permute-done((bf16[1024,1024]{1,0:T(8,128)(2,1)}, bf16[1024,1024]{1,0:T(8,128)(2,1)}, u32[]{:S(2)}, u32[]{:S(2)}) %collective-permute-start.2) | collective-permute-done | bytes 2097184 | tf_op jit(solution)/shard_map/ppermute | solution.py:39
  87.0 3.1 constant_dynamic-update-slice_fusion.7
  90.1 0.0 copy-start
  90.1 3.3 constant_dynamic-update-slice_fusion.6
  93.4 1.5 constant_dynamic-update-slice_fusion.5
  94.9 0.0 copy-done
  94.9 1.5 constant_dynamic-update-slice_fusion.4
  96.4 3.1 constant_dynamic-update-slice_fusion.3
  99.5 3.1 constant_dynamic-update-slice_fusion.2
  102.6 1.5 constant_dynamic-update-slice_fusion.1
  104.1 1.5 constant_dynamic-update-slice_fusion
  105.6 31.6 %all-gather.5.cloned.1.call-done = bf16[4096,1024]{1,0:T(8,128)(2,1)} async-done(((bf16[512,1024]{1,0:T(8,128)(2,1)}), bf16[4096,1024]{1,0:T(8,128)(2,1)}) %all-gather.5.cloned.1.call-update) | async-done | bytes 8388624 | tf_op jit(solution)/shard_map/all_gather | solution.py:47
  137.2 13.8 %fusion.5 = bf16[1024,1024]{0,1:T(8,128)(2,1)S(1)} fusion(bf16[4096,1024]{1,0:T(8,128)(2,1)} %all-gather.5.cloned.1.call-done, bf16[1024,8192]{1,0:T(8,128)(2,1)} %constant_dynamic-update-slice_fusion, s32[]{:T(128)S(6)} %select_n.40), kind=kOutput, calls=%fused_computation.11 | convolution fusion | flops 8590983168 | bytes 18874372 | tf_op jit(solution)/shard_map/dot_general | solution.py:14
  150.9 111.6 %all-gather.7.cloned.1.call-done = bf16[4096,1024]{1,0:T(8,128)(2,1)} async-done(((bf16[512,1024]{1,0:T(8,128)(2,1)}), bf16[4096,1024]{1,0:T(8,128)(2,1)}) %all-gather.7.cloned.1.call-update) | async-done | bytes 8388624 | tf_op jit(solution)/shard_map/all_gather | solution.py:48
  262.5 13.8 %fusion.8 = bf16[1024,1024]{0,1:T(8,128)(2,1)S(1)} fusion(bf16[4096,1024]{1,0:T(8,128)(2,1)} %all-gather.7.cloned.1.call-done, bf16[1024,8192]{1,0:T(8,128)(2,1)} %constant_dynamic-update-slice_fusion, s32[]{:T(128)S(6)} %select_n.40), kind=kOutput, calls=%fused_computation.12 | convolution fusion | flops 8590983168 | bytes 18874372 | tf_op jit(solution)/shard_map/dot_general | solution.py:14
  276.3 2.4 pad_maximum_fusion
  278.7 6.5 %copy.12 = bf16[1024,2048]{1,0:T(8,128)(2,1)} copy(bf16[1024,2048]{0,1:T(8,128)(2,1)} %pad_maximum_fusion) | data formatting | bytes 8388608 | tf_op jit(solution)/shard_map/concatenate | solution.py:49
  285.2 0.0 copy-start.4
  285.2 3.8 gather_fusion
  289.0 3.7 all-to-all-start
  292.8 0.0 copy-done.4
  292.8 0.1 broadcast_compare_fusion
  292.8 3.9 all-gather.9.cloned.1.call-done
  296.8 133.6 %all-gather.11.cloned.1.call-done = bf16[4096,1024]{1,0:T(8,128)(2,1)} async-done(((bf16[512,1024]{1,0:T(8,128)(2,1)}), bf16[4096,1024]{1,0:T(8,128)(2,1)}) %all-gather.11.cloned.1.call-update) | async-done | bytes 8388624 | tf_op jit(solution)/shard_map/all_gather | solution.py:32
  430.4 9.1 %fusion.13 = bf16[64,8,8,128]{3,1,2,0:T(8,128)(2,1)S(1)} fusion(bf16[512,4096]{1,0:T(8,128)(2,1)} %all-gather.9.cloned.1.call-done, bf16[4096,1024]{1,0:T(8,128)(2,1)} %all-gather.11.cloned.1.call-done), kind=kOutput, calls=%fused_computation.17 | convolution fusion | flops 4295491584 | bytes 13631488 | tf_op jit(solution)/shard_map/dot_general | solution.py:14
  439.6 0.3 copy.23
  439.8 0.0 all-to-all-done
  439.9 6.2 %gather_fusion.1 = bf16[128,16,2048]{2,1,0:T(8,128)(2,1)} fusion(bf16[16,16,2048]{2,1,0:T(8,128)(2,1)S(1)} %bitcast.27, s32[1024]{0:T(1024)S(1)} %pad_clamp_fusion), kind=kCustom, calls=%fused_computation.1 | custom fusion | bytes 16777728 | tf_op jit(solution)/shard_map/gather | solution.py:56
  446.1 6.0 %fusion.29 = (bf16[16,128,1024]{2,1,0:T(8,128)(2,1)}, bf16[16,128,1024]{2,1,0:T(8,128)(2,1)}) fusion(bf16[16,128,2048]{2,1,0:T(8,128)(2,1)} %bitcast.28), kind=kLoop, calls=%fused_computation.49 | loop fusion | bytes 16777216 | tf_op jit(solution)/shard_map/slice | solution.py:57
  452.1 6.4 %copy.16 = bf16[16,128,1024]{1,2,0:T(8,128)(2,1)} copy(bf16[16,128,1024]{2,1,0:T(8,128)(2,1)} %get-tuple-element.5) | data formatting | bytes 8388608 | tf_op jit(solution)/shard_map/slice | solution.py:57
  458.5 6.4 %copy.15 = bf16[16,128,1024]{1,2,0:T(8,128)(2,1)} copy(bf16[16,128,1024]{2,1,0:T(8,128)(2,1)} %get-tuple-element.6) | data formatting | bytes 8388608 | tf_op jit(solution)/shard_map/slice | solution.py:58
  464.9 3.4 fusion.14
  468.3 0.0 copy-start.1
  468.3 1.3 copy-done.1
  469.7 1.2 fusion.30
  470.8 10.1 %fusion.12 = bf16[16,32,8,128]{3,1,2,0:T(8,128)(2,1)S(1)} fusion(bf16[16,128,8,128]{1,3,2,0:T(8,128)(2,1)} %bitcast.32, f32[16,8,32]{2,1,0:T(8,128)S(1)} %fusion.30, f32[16,8,32,128]{3,2,1,0:T(8,128)} %copy-done.1, pred[16,128]{1,0:T(8,128)(4,1)S(1)} %broadcast_compare_fusion), kind=kOutput, calls=%fused_computation.16 | convolution fusion | flops 137367680 | bytes 7358464 | tf_op jit(solution)/shard_map/rhgk,rkhe->rghe/dot_general | solution.py:70
  480.9 0.5 copy.20
  481.4 1.2 copy.28
  (5 shorter events, 0.0 us)
Async XLA Ops:
  6.5 54.7 %copy-start.3 = (s32[1,8,2]{1,2,0:T(2,128)S(1)}, s32[1,8,2]{1,2,0:T(2,128)}, u32[]{:S(2)}) copy-start(s32[1,8,2]{1,2,0:T(2,128)} %param.13) | copy-start | bytes 196
  6.5 54.9 %copy-start.2 = (s32[16,8]{0,1:T(8,128)S(1)}, s32[16,8]{0,1:T(8,128)}, u32[]{:S(2)}) copy-start(s32[16,8]{0,1:T(8,128)} %param.14) | copy-start | bytes 1540
  6.5 130.6 %all-gather.5.cloned.1.call-start = ((), (), s32[]{:S(2)}) async-start(), calls=%async_computation.1 | async-start | bytes 9437184 | tf_op jit(solution)/shard_map/all_gather | solution.py:47
  7.3 255.3 %all-gather.7.cloned.1.call-start = ((), (), s32[]{:S(2)}) async-start(), calls=%async_computation.2 | async-start | bytes 9437184 | tf_op jit(solution)/shard_map/all_gather | solution.py:48
  8.0 288.8 %all-gather.9.cloned.1.call-start = ((), (), s32[]{:S(2)}) async-start(), calls=%async_computation.3 | async-start | bytes 5242880 | tf_op jit(solution)/shard_map/all_gather | solution.py:31
  8.7 421.7 %all-gather.11.cloned.1.call-start = ((), (), s32[]{:S(2)}) async-start(), calls=%async_computation.4 | async-start | bytes 9437184 | tf_op jit(solution)/shard_map/all_gather | solution.py:32
  9.3 26.4 %collective-permute-start = (bf16[1024,1024]{1,0:T(8,128)(2,1)}, bf16[1024,1024]{1,0:T(8,128)(2,1)S(1)}, u32[]{:S(2)}, u32[]{:S(2)}) collective-permute-start(bf16[1024,1024]{1,0:T(8,128)(2,1)} %param.9), channel_id=1, source_target_pairs={{0,1},{1,2},{2,3},{3,0},{4,5},{5,6},{6,7},{7,4},{8,9},{9,10},{10,1... | collective-permute-start | bytes 6291464 | tf_op jit(solution)/shard_map/ppermute | solution.py:39
  35.7 25.6 %collective-permute-start.1 = (bf16[1024,1024]{1,0:T(8,128)(2,1)S(1)}, bf16[1024,1024]{1,0:T(8,128)(2,1)}, u32[]{:S(2)}, u32[]{:S(2)}) collective-permute-start(bf16[1024,1024]{1,0:T(8,128)(2,1)S(1)} %collective-permute-done), channel_id=1, source_target_pairs={{0,1},{1,2},{2,3},{3,0},{4,5},{5,6},{6,7},{7,4},{8,9},{9,10},{10,1... | collective-permute-start | bytes 6291464 | tf_op jit(solution)/shard_map/ppermute | solution.py:39
  61.2 25.8 %collective-permute-start.2 = (bf16[1024,1024]{1,0:T(8,128)(2,1)}, bf16[1024,1024]{1,0:T(8,128)(2,1)}, u32[]{:S(2)}, u32[]{:S(2)}) collective-permute-start(bf16[1024,1024]{1,0:T(8,128)(2,1)} %collective-permute-done.1), channel_id=1, source_target_pairs={{0,1},{1,2},{2,3},{3,0},{4,5},{5,6},{6,7},{7,4},{8,9},{9,10},{10,1... | collective-permute-start | bytes 6291464 | tf_op jit(solution)/shard_map/ppermute | solution.py:39
  90.1 4.8 copy-start
  285.2 7.5 %copy-start.4 = (s32[16]{0:T(128)S(1)}, s32[16]{0:T(128)}, u32[]{:S(2)}) copy-start(s32[16]{0:T(128)} %param.15) | copy-start | bytes 196
  289.0 150.8 %all-to-all-start = ((bf16[8,2,16,2048]{3,2,1,0:T(8,128)(2,1)}), bf16[8,2,16,2048]{3,2,1,0:T(8,128)(2,1)S(1)}, u32[]{:S(2)}, u32[]{:S(2)}) async-start(bf16[8,2,16,2048]{3,2,1,0:T(8,128)(2,1)} %bitcast.2), calls=%async_computation | async-start | bytes 2097152 | tf_op jit(solution)/shard_map/all_to_all | solution.py:54
  468.3 1.3 copy-start.1
Sparse Core Ops, SparseCore 0:
  9.5 127.6 all-gather.4
  139.3 123.1 all-gather.6
  264.1 32.6 all-gather.8
  298.8 131.6 all-gather.10
